TPU v7x, 512 devices: a whole 4x8x8 slice. The times are simulated.
512 devices in a mesh: segment: 4 (over z_lo), seq: 16 (over z_hi, x, core), mp: 8 (over y).
Axes of the slice: x: 4, y: 8, z: 8 (z_hi: 2, z_lo: 4; z = z_hi * 4 + z_lo), core: 2. Of those that a mesh axis runs over, the one named last changes fastest.
Arguments:
- latents: bfloat16 [4, 16, 256, 4096], P('segment', 'seq', None, 'mp'), may hold values from -6 to 6
- w_qkv: bfloat16 [4, 4096, 3, 4096], P('segment', 'seq', None, 'mp'), may hold values from -1 to 1
- w_out: bfloat16 [4, 4096, 4096], P('segment', 'mp', 'seq'), may hold values from -0.09375 to 0.09375
- mod_shift: float32 [4, 4096], P('segment'), may hold values from -3 to 3
- mod_scale: float32 [4, 4096], P('segment'), may hold values from 0.1 to 1.9
- mod_gate: float32 [4, 4096], P('segment'), may hold values from 0.5 to 1.5
- counts: int32 [4, 16], P('segment'), may hold values from 64 to 256, as said below
Outputs:
- next_latents: bfloat16 [4, 16, 256, 4096], P('segment', 'seq', None, 'mp')
Inputs may be any that keep to these rules, and one draw needn't show every extreme that they name: `counts`: in every section's clip at least one frame has all 256 patch positions valid.
All inputs are finite; a program needn't handle non-finite values.
Results may differ from a plain program's by a relative error of at most 0.01.
Values may be sent and summed in bfloat16 or wider, within the bound.
No kernel may reach another device: no remote copies, remote signals or barrier semaphores. Data moves between devices by JAX's collectives and lax.ppermute only.
A program may use at most 64 MiB of HBM per device.

v0:
```python
import math
import jax
import jax.numpy as jnp
from jax import lax
from jax.sharding import PartitionSpec as P

HD = 128
EPS = 1e-06
NEG_FILL = -1e30


def passed_along(x, axis, by):
    length = lax.axis_size(axis)
    return lax.ppermute(x, axis, [(i, (i + by) % length) for i in range(length)])


def masked_attention(queries, keys_in, values, usable):
    factor = 1.0 / math.sqrt(queries.shape[-1])
    scores = (
        jnp.einsum("...ihe,...jhe->...hij", queries, keys_in, preferred_element_type=jnp.float32)
        * factor
    )
    allowed = usable[..., None, :, None] & usable[..., None, None, :]
    masked = jnp.where(allowed, scores, NEG_FILL)
    highest = jnp.max(masked, axis=-1, keepdims=True)
    raised = jnp.where(allowed, jnp.exp(masked - highest), 0.0)
    spare_one = jnp.where(usable, 0.0, 1.0)[..., None, :, None]
    weights = (raised / (jnp.sum(raised, axis=-1, keepdims=True) + spare_one)).astype(jnp.bfloat16)
    blended = jnp.einsum(
        "...hij,...jhe->...ihe", weights, values, preferred_element_type=jnp.float32
    )
    return blended.astype(jnp.bfloat16)


def relay_features(rows_now):
    return lax.all_to_all(rows_now, "seq", split_axis=0, concat_axis=0, tiled=True)


def pass_onward(rows_now):
    return passed_along(rows_now, "segment", 1)


def on_device(latents, w_qkv, w_out, mod_shift, mod_scale, mod_gate, counts):
    frames = lax.axis_size("seq")
    patches = latents.shape[2]
    narrow = latents.shape[3]
    span = patches // frames
    segment_rows = latents[0, 0]
    gathered = lax.all_gather(latents, "mp", axis=3, tiled=True)[0, 0]
    widened = gathered.astype(jnp.float32)
    average = jnp.mean(widened, axis=-1, keepdims=True)
    centred = widened - average
    variance = jnp.mean(centred * centred, axis=-1, keepdims=True)
    modulated = (centred * lax.rsqrt(variance + EPS) * mod_scale[0] + mod_shift[0]).astype(
        jnp.bfloat16
    )
    columns = w_qkv.shape[2] * w_qkv.shape[3]
    piece = lax.all_gather(w_qkv, "seq", axis=1, tiled=True)
    height = piece.shape[1]
    projected = jnp.dot(
        modulated, piece.reshape(height, columns), preferred_element_type=jnp.float32
    )
    local_heads = w_qkv.shape[3] // HD
    projected = projected.astype(jnp.bfloat16).reshape(patches, 3, local_heads, HD)
    frame_here = lax.axis_index("seq")
    clip_counts = counts[0]
    positions = jnp.arange(frames)

    def spatial(triple):
        count_here = jnp.sum(jnp.where(positions == frame_here, clip_counts, 0))
        usable = jnp.arange(patches) < count_here
        return masked_attention(triple[:, 0], triple[:, 1], triple[:, 2], usable)

    def temporal(triple):
        by_place = triple.reshape(frames, span, 3, local_heads, HD).transpose(1, 0, 2, 3, 4)
        location = frame_here * span + jnp.arange(span)
        usable = location[:, None] < clip_counts[None, :]
        blended = masked_attention(by_place[:, :, 0], by_place[:, :, 1], by_place[:, :, 2], usable)
        return blended.transpose(1, 0, 2, 3).reshape(patches, local_heads, HD)

    attended = lax.cond(lax.axis_index("segment") % 2 == 0, spatial, temporal, projected)
    attended = attended.reshape(patches, local_heads * HD)
    out_whole = lax.all_gather(w_out, "seq", axis=2, tiled=True)[0]
    member = lax.axis_index("mp")
    partials = jnp.dot(attended, out_whole, preferred_element_type=jnp.float32)
    summed = lax.psum_scatter(
        partials.astype(jnp.bfloat16), "mp", scatter_dimension=1, tiled=True
    ).astype(jnp.float32)
    gate_here = lax.dynamic_slice_in_dim(mod_gate[0], member * narrow, narrow)
    updated = (segment_rows.astype(jnp.float32) + gate_here * summed).astype(jnp.bfloat16)
    updated = updated.reshape(frames, span, narrow)
    moved = pass_onward(relay_features(updated))
    return moved.reshape(1, 1, patches, narrow)


def solution(mesh):
    return jax.shard_map(
        on_device,
        mesh=mesh,
        in_specs=(
            P("segment", "seq", None, "mp"),
            P("segment", "seq", None, "mp"),
            P("segment", "mp", "seq"),
            P("segment", None),
            P("segment", None),
            P("segment", None),
            P("segment", None),
        ),
        out_specs=P("segment", "seq", None, "mp"),
        check_vma=False,
    )
```

profile of v0, /device:TPU:1, one launch (start us, length us, event | category | flops | bytes accessed | tf_op | source)
XLA Modules:
  0.0 384.6 jit_solution(8186895898152812026)
XLA Ops:
  6.5 0.0 copy-start
  6.5 0.0 copy-start.5
  6.5 0.0 copy-start.4
  6.5 0.0 all-gather.4.cloned.1.call-start
  6.5 0.7 all-gather.4.cloned.1.call-update
  7.3 0.0 all-gather.6.cloned.1.call-start
  7.3 2.3 copy.18
  9.6 0.0 all-gather.6.cloned.1.call-update
  9.7 0.0 all-gather.8.cloned.1.call-start
  9.7 0.7 all-gather.8.cloned.1.call-update
  10.4 0.0 reduce-scatter.2.cloned.1.call-start
  10.5 43.7 %all-gather.4.cloned.1.call-done = bf16[1,1,256,4096]{3,2,1,0:T(8,128)(2,1)} async-done(((bf16[1,1,256,512]{3,2,1,0:T(8,128)(2,1)}), bf16[1,1,256,4096]{3,2,1,0:T(8,128)(2,1)}) %all-gather.4.cloned.1.call-update) | async-done | bytes 2097168 | tf_op jit(solution)/shard_map/all_gather | solution.py:49
  54.1 0.0 copy-start.1
  54.1 2.1 convert_reduce_fusion
  56.2 2.3 fusion.30
  58.5 157.1 %all-gather.6.cloned.1.call-done = bf16[1,4096,3,512]{1,3,2,0:T(8,128)(2,1)} async-done(((bf16[1,256,3,512]{1,3,2,0:T(8,128)(2,1)}), bf16[1,4096,3,512]{1,3,2,0:T(8,128)(2,1)}) %all-gather.6.cloned.1.call-update) | async-done | bytes 12582928 | tf_op jit(solution)/shard_map/all_gather | solution.py:58
  215.6 0.0 copy-done.5
  215.6 0.0 copy-done.4
  215.6 0.0 copy-done.1
  215.7 0.0 copy-start.3
  215.7 8.2 %convolution_convert_fusion.3 = bf16[256,1536]{1,0:T(8,128)(2,1)S(1)} fusion(bf16[4096,1536]{0,1:T(8,128)(2,1)} %bitcast.96, bf16[1,1,256,4096]{3,2,1,0:T(8,128)(2,1)S(1)} %copy-done.1, f32[4096]{0:T(1024)S(1)} %bitcast.97, f32[4096]{0:T(1024)S(1)} %bitcast.98, f32[256]{0:T(256)S(1)} %add_rsqrt_fusion, f32[256]{0:T(256)S(1)} %broadcast_multiply_fusion), kind=kOutput, calls=%fused_computation.58 | convolution fusion | flops 3227910144 | bytes 15501312 | tf_op jit(solution)/shard_map/dot_general | solution.py:60
  223.9 0.0 copy-done.3
  223.9 3.7 conditional.1
  223.9 0.6 fusion.14
  224.6 0.6 iota_compare_fusion
  225.1 0.1 broadcast_and_fusion.1
  225.2 0.3 copy.19
  225.5 0.6 fusion.40
  226.2 0.6 broadcast_select_fusion.1
  226.7 0.8 convolution_convert_fusion.1
  227.6 0.0 copy-start.2
  227.6 71.0 %all-gather.8.cloned.1.call-done = bf16[1,512,4096]{2,1,0:T(8,128)(2,1)} async-done(((bf16[1,512,256]{2,1,0:T(8,128)(2,1)}), bf16[1,512,4096]{2,1,0:T(8,128)(2,1)}) %all-gather.8.cloned.1.call-update) | async-done | bytes 4194320 | tf_op jit(solution)/shard_map/all_gather | solution.py:83
  298.5 4.8 %convolution_convert_fusion.2 = bf16[256,4096]{1,0:T(8,128)(2,1)} fusion(bf16[256,512]{0,1:T(8,128)(2,1)S(1)} %get-tuple-element.36, bf16[1,512,4096]{2,1,0:T(8,128)(2,1)} %all-gather.8.cloned.1.call-done), kind=kOutput, calls=%fused_computation.49 | convolution fusion | flops 1074790400 | bytes 6553600 | tf_op jit(solution)/shard_map/dot_general | solution.py:85
  303.4 0.0 reduce-scatter.2.cloned.1.call-update
  303.4 0.0 copy-done
  303.4 36.3 %reduce-scatter.2.cloned.1.call-done = bf16[256,512]{1,0:T(8,128)(2,1)} async-done(((bf16[256,4096]{1,0:T(8,128)(2,1)}), bf16[256,512]{1,0:T(8,128)(2,1)}) %reduce-scatter.2.cloned.1.call-update) | async-done | bytes 262160 | tf_op jit(solution)/shard_map/reduce_scatter | solution.py:86
  339.7 0.0 copy-done.2
  339.7 1.0 fusion.38
  340.7 26.0 %all_to_all.5 = bf16[16,16,512]{2,1,0:T(8,128)(2,1)S(1)} all-to-all(bf16[16,16,512]{2,1,0:T(8,128)(2,1)S(1)} %bitcast.84), channel_id=1, replica_groups=mesh['segment'=4,'seq'=16,'mp'=8] {'seq'}, dimensions={0} | all-to-all | bytes 524288 | tf_op jit(solution)/shard_map/all_to_all | solution.py:36
  366.8 5.0 %collective-permute-start = (bf16[16,16,512]{2,1,0:T(8,128)(2,1)S(1)}, bf16[16,16,512]{2,1,0:T(8,128)(2,1)S(1)}, u32[]{:S(2)}, u32[]{:S(2)}) collective-permute-start(bf16[16,16,512]{2,1,0:T(8,128)(2,1)S(1)} %all_to_all.5), channel_id=1, source_target_pairs={{0,128},{128,256},{256,384},{384,0},{1,129},{129,257},{257,385},{3... | collective-permute-start | bytes 786440 | tf_op jit(solution)/shard_map/ppermute | solution.py:14
  371.7 5.6 %collective-permute-done = bf16[16,16,512]{2,1,0:T(8,128)(2,1)S(1)} collective-permute-done((bf16[16,16,512]{2,1,0:T(8,128)(2,1)S(1)}, bf16[16,16,512]{2,1,0:T(8,128)(2,1)S(1)}, u32[]{:S(2)}, u32[]{:S(2)}) %collective-permute-start) | collective-permute-done | bytes 262176 | tf_op jit(solution)/shard_map/ppermute | solution.py:14
  377.4 0.7 copy.32
  (5 shorter events, 0.0 us)
Async XLA Ops:
  6.5 296.9 %copy-start = (f32[1,4096]{1,0:T(1,128)S(1)}, f32[1,4096]{1,0:T(1,128)}, u32[]{:S(2)}) copy-start(f32[1,4096]{1,0:T(1,128)} %param.14) | copy-start | bytes 49156
  6.5 209.1 %copy-start.5 = (f32[1,4096]{1,0:T(1,128)S(1)}, f32[1,4096]{1,0:T(1,128)}, u32[]{:S(2)}) copy-start(f32[1,4096]{1,0:T(1,128)} %param.13) | copy-start | bytes 49156
  6.5 209.1 %copy-start.4 = (f32[1,4096]{1,0:T(1,128)S(1)}, f32[1,4096]{1,0:T(1,128)}, u32[]{:S(2)}) copy-start(f32[1,4096]{1,0:T(1,128)} %param.12) | copy-start | bytes 49156
  6.5 47.6 %all-gather.4.cloned.1.call-start = ((), (), s32[]{:S(2)}) async-start(), calls=%async_computation.2 | async-start | bytes 2359296 | tf_op jit(solution)/shard_map/all_gather | solution.py:49
  7.3 208.4 %all-gather.6.cloned.1.call-start = ((), (), s32[]{:S(2)}) async-start(), calls=%async_computation.3 | async-start | bytes 13369344 | tf_op jit(solution)/shard_map/all_gather | solution.py:58
  9.7 288.9 %all-gather.8.cloned.1.call-start = ((), (), s32[]{:S(2)}) async-start(), calls=%async_computation.4 | async-start | bytes 4456448 | tf_op jit(solution)/shard_map/all_gather | solution.py:83
  10.4 329.3 %reduce-scatter.2.cloned.1.call-start = ((), (), s32[]{:S(2)}) async-start(), calls=%async_computation.5 | async-start | bytes 2359296 | tf_op jit(solution)/shard_map/reduce_scatter | solution.py:86
  54.1 161.5 %copy-start.1 = (bf16[1,1,256,4096]{3,2,1,0:T(8,128)(2,1)S(1)}, bf16[1,1,256,4096]{3,2,1,0:T(8,128)(2,1)}, u32[]{:S(2)}) copy-start(bf16[1,1,256,4096]{3,2,1,0:T(8,128)(2,1)} %all-gather.4.cloned.1.call-done) | copy-start | bytes 6291460
  215.7 8.3 %copy-start.3 = (s32[1,16]{1,0:T(1,128)S(1)}, s32[1,16]{1,0:T(1,128)}, u32[]{:S(2)}) copy-start(s32[1,16]{1,0:T(1,128)} %param.15) | copy-start | bytes 196
  227.6 112.1 %copy-start.2 = (bf16[1,1,256,512]{3,2,1,0:T(8,128)(2,1)S(1)}, bf16[1,1,256,512]{3,2,1,0:T(8,128)(2,1)}, u32[]{:S(2)}) copy-start(bf16[1,1,256,512]{3,2,1,0:T(8,128)(2,1)} %param.9) | copy-start | bytes 786436
  366.8 10.6 %collective-permute-start = (bf16[16,16,512]{2,1,0:T(8,128)(2,1)S(1)}, bf16[16,16,512]{2,1,0:T(8,128)(2,1)S(1)}, u32[]{:S(2)}, u32[]{:S(2)}) collective-permute-start(bf16[16,16,512]{2,1,0:T(8,128)(2,1)S(1)} %all_to_all.5), channel_id=1, source_target_pairs={{0,128},{128,256},{256,384},{384,0},{1,129},{129,257},{257,385},{3... | collective-permute-start | bytes 786440 | tf_op jit(solution)/shard_map/ppermute | solution.py:14
Sparse Core Ops, SparseCore 0:
  9.4 44.6 all-gather.3
  57.3 158.3 all-gather.5
  218.8 79.7 all-gather.7
  303.5 36.1 reduce-scatter.1
where the time goes:
time: 385 us
  waiting for transfers between devices  315 us (82%)
  blocking collectives  26 us (7%)
  matrix products  14.5 us (4%)
  between operations  13.2 us (3%)
  other arithmetic  7.29 us (2%)
  starting transfers between devices  5.07 us (1%)
    all_gather x1, waiting for transfers between devices, on_device(): piece = lax.all_gather(w_qkv, 'seq', axis=1, tiled=True)  157 us
    all_gather x1, waiting for transfers between devices, on_device(): out_whole = lax.all_gather(w_out, 'seq', axis=2, tiled=True)[0]  71 us
    all_gather x1, waiting for transfers between devices, on_device(): gathered = lax.all_gather(latents, 'mp', axis=3, tiled=True)[0, 0]  43.7 us
    reduce_scatter x1, waiting for transfers between devices, on_device(): lax.psum_scatter(partials.astype(jnp.bfloat16), 'mp', scatter_dimension=1...  36.3 us
    all_to_all x1, blocking collectives, relay_features(): lax.all_to_all(rows_now, 'seq', split_axis=0, concat_axis=0, tiled=True)  26 us
    dot_general x1, matrix products, on_device(): jnp.dot(modulated, piece.reshape(height, columns), preferred_element_type...  8.22 us
  transfers between devices with their start and end apart: 5, of which 5 were waited for; matrix products, arithmetic and copies ran while one was open for 5% of the time, Pallas kernels for 0%

commit v1 on v0

--- a/solution.py
+++ b/solution.py
@@ -46,7 +46,9 @@
     narrow = latents.shape[3]
     span = patches // frames
     segment_rows = latents[0, 0]
-    gathered = lax.all_gather(latents, "mp", axis=3, tiled=True)[0, 0]
+    gathered = jnp.concatenate(
+        lax.all_to_all(jnp.stack([latents] * lax.axis_size("mp")), "mp", 0, 0), axis=3
+    )[0, 0]
     widened = gathered.astype(jnp.float32)
     average = jnp.mean(widened, axis=-1, keepdims=True)
     centred = widened - average

time: 385 us -> 341 us (0.89)
  waiting for transfers between devices: 315 us -> 259 us
  starting transfers between devices: 5.07 us -> 12.5 us
    all_gather x1, waiting for transfers between devices: 157 us -> 96 us  [on_device(): piece = lax.all_gather(w_qkv, 'seq', axis=1, tiled=True)]
    all_to_all x0 -> x1, waiting for transfers between devices: none -> 49.8 us  [on_device(): lax.all_to_all(jnp.stack([latents] * lax.axis_size('mp')), 'mp', 0, 0)]
    all_gather x1 -> x0, waiting for transfers between devices: 43.7 us -> none  [on_device(): gathered = lax.all_gather(latents, 'mp', axis=3, tiled=True)[0, 0]]
    all_to_all x0 -> x1, starting transfers between devices: none -> 7.64 us  [on_device(): lax.all_to_all(jnp.stack([latents] * lax.axis_size('mp')), 'mp', 0, 0)]
  transfers between devices with their start and end apart: 5 -> 5, of which waited for: 5 -> 5; matrix products, arithmetic and copies ran while one was open for 5% -> 6% of each run, Pallas kernels for 0% -> 0%
where the time goes in v1:
time: 341 us; the launch traced here: 340 us
  waiting for transfers between devices  259 us (76%)
  blocking collectives  26 us (8%)
  matrix products  15 us (4%)
  between operations  13.2 us (4%)
  starting transfers between devices  12.5 us (4%)
  other arithmetic  7.95 us (2%)
  local copies, waits for them, and re-layouts  6.42 us (2%)
    all_gather x1, waiting for transfers between devices, on_device(): piece = lax.all_gather(w_qkv, 'seq', axis=1, tiled=True)  96 us
    all_gather x1, waiting for transfers between devices, on_device(): out_whole = lax.all_gather(w_out, 'seq', axis=2, tiled=True)[0]  70.5 us
    all_to_all x1, waiting for transfers between devices, on_device(): lax.all_to_all(jnp.stack([latents] * lax.axis_size('mp')), 'mp', 0, 0)  49.8 us
    reduce_scatter x1, waiting for transfers between devices, on_device(): lax.psum_scatter(partials.astype(jnp.bfloat16), 'mp', scatter_dimension=1...  36.3 us
    all_to_all x1, blocking collectives, relay_features(): lax.all_to_all(rows_now, 'seq', split_axis=0, concat_axis=0, tiled=True)  26 us
    dot_general x1, matrix products, on_device(): jnp.dot(modulated, piece.reshape(height, columns), preferred_element_type...  8.7 us
    all_to_all x1, starting transfers between devices, on_device(): lax.all_to_all(jnp.stack([latents] * lax.axis_size('mp')), 'mp', 0, 0)  7.64 us
  transfers between devices with their start and end apart: 5, of which 5 were waited for; matrix products, arithmetic and copies ran while one was open for 6% of the time, Pallas kernels for 0%

profile of v1, /device:TPU:1, one launch (start us, length us, event | category | flops | bytes accessed | tf_op | source)
XLA Modules:
  0.0 340.3 jit_solution(16280349817697929757)
XLA Ops:
  6.5 0.0 copy-start
  6.5 0.0 all-gather.3.cloned.1.call-start
  6.5 2.3 copy.30
  8.9 0.0 copy-start.2
  8.9 0.0 copy-start.3
  8.9 0.0 all-gather.3.cloned.1.call-update
  8.9 0.0 all-gather.5.cloned.1.call-start
  8.9 0.7 all-gather.5.cloned.1.call-update
  9.7 1.1 copy.28
  10.7 1.5 stack.2
  12.2 7.6 %all-to-all-start = ((bf16[8,1,1,256,512]{3,4,2,1,0:T(8,128)(2,1)}), bf16[8,1,1,256,512]{3,4,2,1,0:T(8,128)(2,1)S(1)}, u32[]{:S(2)}, u32[]{:S(2)}) async-start(bf16[8,1,1,256,512]{3,4,2,1,0:T(8,128)(2,1)} %stack.2), calls=%async_computation | async-start | bytes 4194304 | tf_op jit(solution)/shard_map/all_to_all | solution.py:50
  19.9 0.0 reduce-scatter.2.cloned.1.call-start
  19.9 0.5 broadcast.210
  20.4 0.0 copy-done.2
  20.4 0.6 reduce.10
  21.1 0.0 copy-done.3
  21.1 0.6 reduce.11
  21.7 49.8 %all-to-all-done = bf16[8,1,1,256,512]{3,4,2,1,0:T(8,128)(2,1)S(1)} async-done(((bf16[8,1,1,256,512]{3,4,2,1,0:T(8,128)(2,1)}), bf16[8,1,1,256,512]{3,4,2,1,0:T(8,128)(2,1)S(1)}, u32[]{:S(2)}, u32[]{:S(2)}) %all-to-all-start) | async-done | bytes 2097184 | tf_op jit(solution)/shard_map/all_to_all | solution.py:50
  71.5 0.6 convert_reduce_fusion
  72.1 0.6 fusion.26
  72.7 2.7 fusion.29
  75.4 96.0 %all-gather.3.cloned.1.call-done = bf16[1,4096,3,512]{1,3,2,0:T(8,128)(2,1)} async-done(((bf16[1,256,3,512]{1,3,2,0:T(8,128)(2,1)}), bf16[1,4096,3,512]{1,3,2,0:T(8,128)(2,1)}) %all-gather.3.cloned.1.call-update) | async-done | bytes 12582928 | tf_op jit(solution)/shard_map/all_gather | solution.py:60
  171.4 0.0 copy-start.4
  171.4 8.7 %convolution_convert_fusion.3 = bf16[256,1536]{1,0:T(8,128)(2,1)S(1)} fusion(bf16[256,4096]{0,1:T(8,128)(2,1)} %bitcast.78, bf16[4096,1536]{0,1:T(8,128)(2,1)} %bitcast.92), kind=kOutput, calls=%fused_computation.56 | convolution fusion | flops 3221618688 | bytes 15466496 | tf_op jit(solution)/shard_map/dot_general | solution.py:62
  180.1 0.0 copy-done.4
  180.1 3.7 %conditional.1 = (bf16[256,512]{0,1:T(8,128)(2,1)S(1)}) conditional(s32[]{:T(128)} %convert_element_type.51, (s32[]{:T(128)}, s32[1,16]{1,0:T(1,128)S(1)}, bf16[256,1536]{1,0:T(8,128)(2,1)S(1)}) %tuple.25, (s32[]{:T(128)}, s32[16]{0:T(128)S(1)}, s32[1,16]{1,0:T(1,128)S(1)}, bf16[256,1536]{1,0:T(8,128)(2,1)S(1)}) %tuple.26), branch_computations={%region_2.5_spmd, %region_5.9_spmd} | conditional | flops 204410160 | bytes 6552408 | solution.py:83
  180.1 0.6 fusion.14
  180.8 0.6 iota_compare_fusion
  181.3 0.1 broadcast_and_fusion.1
  181.4 0.3 copy.31
  181.7 0.6 fusion.32
  182.4 0.6 broadcast_select_fusion.1
  183.0 0.8 convolution_convert_fusion.1
  183.8 0.0 copy-start.1
  183.8 70.5 %all-gather.5.cloned.1.call-done = bf16[1,512,4096]{2,1,0:T(8,128)(2,1)} async-done(((bf16[1,512,256]{2,1,0:T(8,128)(2,1)}), bf16[1,512,4096]{2,1,0:T(8,128)(2,1)}) %all-gather.5.cloned.1.call-update) | async-done | bytes 4194320 | tf_op jit(solution)/shard_map/all_gather | solution.py:85
  254.3 4.8 %convolution_convert_fusion.2 = bf16[256,4096]{1,0:T(8,128)(2,1)} fusion(bf16[256,512]{0,1:T(8,128)(2,1)S(1)} %get-tuple-element.40, bf16[1,512,4096]{2,1,0:T(8,128)(2,1)} %all-gather.5.cloned.1.call-done), kind=kOutput, calls=%fused_computation.48 | convolution fusion | flops 1074790400 | bytes 6553600 | tf_op jit(solution)/shard_map/dot_general | solution.py:87
  259.1 0.0 reduce-scatter.2.cloned.1.call-update
  259.1 0.0 copy-done
  259.2 36.3 %reduce-scatter.2.cloned.1.call-done = bf16[256,512]{1,0:T(8,128)(2,1)} async-done(((bf16[256,4096]{1,0:T(8,128)(2,1)}), bf16[256,512]{1,0:T(8,128)(2,1)}) %reduce-scatter.2.cloned.1.call-update) | async-done | bytes 262160 | tf_op jit(solution)/shard_map/reduce_scatter | solution.py:88
  295.4 0.0 copy-done.1
  295.4 1.0 add_convert_fusion
  296.5 26.0 %all_to_all.10 = bf16[16,16,512]{2,1,0:T(8,128)(2,1)S(1)} all-to-all(bf16[16,16,512]{2,1,0:T(8,128)(2,1)S(1)} %bitcast.80), channel_id=1, replica_groups=mesh['segment'=4,'seq'=16,'mp'=8] {'seq'}, dimensions={0} | all-to-all | bytes 524288 | tf_op jit(solution)/shard_map/all_to_all | solution.py:36
  322.5 4.8 %collective-permute-start = (bf16[16,16,512]{2,1,0:T(8,128)(2,1)S(1)}, bf16[16,16,512]{2,1,0:T(8,128)(2,1)S(1)}, u32[]{:S(2)}, u32[]{:S(2)}) collective-permute-start(bf16[16,16,512]{2,1,0:T(8,128)(2,1)S(1)} %all_to_all.10), channel_id=1, source_target_pairs={{0,128},{128,256},{256,384},{384,0},{1,129},{129,257},{257,385},{3... | collective-permute-start | bytes 786440 | tf_op jit(solution)/shard_map/ppermute | solution.py:14
  327.3 5.8 %collective-permute-done = bf16[16,16,512]{2,1,0:T(8,128)(2,1)S(1)} collective-permute-done((bf16[16,16,512]{2,1,0:T(8,128)(2,1)S(1)}, bf16[16,16,512]{2,1,0:T(8,128)(2,1)S(1)}, u32[]{:S(2)}, u32[]{:S(2)}) %collective-permute-start) | collective-permute-done | bytes 262176 | tf_op jit(solution)/shard_map/ppermute | solution.py:14
  333.1 0.7 copy.44
  (7 shorter events, 0.0 us)
Async XLA Ops:
  6.5 252.6 %copy-start = (f32[1,4096]{1,0:T(1,128)S(1)}, f32[1,4096]{1,0:T(1,128)}, u32[]{:S(2)}) copy-start(f32[1,4096]{1,0:T(1,128)} %param.14) | copy-start | bytes 49156
  6.5 164.9 %all-gather.3.cloned.1.call-start = ((), (), s32[]{:S(2)}) async-start(), calls=%async_computation.3 | async-start | bytes 13369344 | tf_op jit(solution)/shard_map/all_gather | solution.py:60
  8.9 11.6 %copy-start.2 = (f32[1,4096]{1,0:T(1,128)S(1)}, f32[1,4096]{1,0:T(1,128)}, u32[]{:S(2)}) copy-start(f32[1,4096]{1,0:T(1,128)} %param.12) | copy-start | bytes 49156
  8.9 12.2 %copy-start.3 = (f32[1,4096]{1,0:T(1,128)S(1)}, f32[1,4096]{1,0:T(1,128)}, u32[]{:S(2)}) copy-start(f32[1,4096]{1,0:T(1,128)} %param.13) | copy-start | bytes 49156
  8.9 245.4 %all-gather.5.cloned.1.call-start = ((), (), s32[]{:S(2)}) async-start(), calls=%async_computation.4 | async-start | bytes 4456448 | tf_op jit(solution)/shard_map/all_gather | solution.py:85
  12.2 59.3 %all-to-all-start = ((bf16[8,1,1,256,512]{3,4,2,1,0:T(8,128)(2,1)}), bf16[8,1,1,256,512]{3,4,2,1,0:T(8,128)(2,1)S(1)}, u32[]{:S(2)}, u32[]{:S(2)}) async-start(bf16[8,1,1,256,512]{3,4,2,1,0:T(8,128)(2,1)} %stack.2), calls=%async_computation | async-start | bytes 4194304 | tf_op jit(solution)/shard_map/all_to_all | solution.py:50
  19.9 275.6 %reduce-scatter.2.cloned.1.call-start = ((), (), s32[]{:S(2)}) async-start(), calls=%async_computation.5 | async-start | bytes 2359296 | tf_op jit(solution)/shard_map/reduce_scatter | solution.py:88
  171.4 8.7 %copy-start.4 = (s32[1,16]{1,0:T(1,128)S(1)}, s32[1,16]{1,0:T(1,128)}, u32[]{:S(2)}) copy-start(s32[1,16]{1,0:T(1,128)} %param.15) | copy-start | bytes 196
  183.8 111.7 %copy-start.1 = (bf16[1,1,256,512]{3,2,1,0:T(8,128)(2,1)S(1)}, bf16[1,1,256,512]{3,2,1,0:T(8,128)(2,1)}, u32[]{:S(2)}) copy-start(bf16[1,1,256,512]{3,2,1,0:T(8,128)(2,1)} %param.9) | copy-start | bytes 786436
  322.5 10.6 %collective-permute-start = (bf16[16,16,512]{2,1,0:T(8,128)(2,1)S(1)}, bf16[16,16,512]{2,1,0:T(8,128)(2,1)S(1)}, u32[]{:S(2)}, u32[]{:S(2)}) collective-permute-start(bf16[16,16,512]{2,1,0:T(8,128)(2,1)S(1)} %all_to_all.10), channel_id=1, source_target_pairs={{0,128},{128,256},{256,384},{384,0},{1,129},{129,257},{257,385},{3... | collective-permute-start | bytes 786440 | tf_op jit(solution)/shard_map/ppermute | solution.py:14
Sparse Core Ops, SparseCore 0:
  10.5 160.8 all-gather.2
  174.5 79.7 all-gather.4
  259.2 36.1 reduce-scatter.1
